TPU v7x, 32 devices: a whole 2x2x4 slice. The times are simulated.
32 devices in a mesh: blk: 8 (over z, core), grp: 4 (over y, x).
Axes of the slice: x: 2, y: 2, z: 4, core: 2. Of those that a mesh axis runs over, the one named last changes fastest.
Arguments:
- block_values: bfloat16 [1536, 16, 64, 64], P('blk', 'grp'), may hold values from -1.5 to 1.5
- block_columns: int32 [1536, 16], P('blk', 'grp'), may hold values from 0 to 1535, as said below
- row_counts: int32 [1536], P('blk'), may hold values from 6 to 16
- prolong_blocks: bfloat16 [1536, 64, 64], P(('blk', 'grp')), may hold values from -0.75 to 0.75
- aggregates: int32 [1536], P(('blk', 'grp')), may hold values from 0 to 31, as said below
Outputs:
- coarse_blocks: float32 [32, 32, 64, 64], P('grp', 'blk')
Inputs may be any that keep to these rules, and one draw needn't show every extreme that they name: `aggregates`: the aggregate of a fine block row of panel p, rows p * 192 to (p + 1) * 192 - 1, lies in p * 4 to (p + 1) * 4 - 1. `block_columns`: A block column of a row of panel p lies in a panel p + d modulo the number of panels, for some d of -2 to 2; slot 0 of each row holds the row itself.
All inputs are finite; a program needn't handle non-finite values.
Results may differ from a plain program's by a relative error of at most 0.0029.
Values may be sent and summed in bfloat16 or wider, within the bound.
No kernel may reach another device: no remote copies, remote signals or barrier semaphores. Data moves between devices by JAX's collectives and lax.ppermute only.
A program may use at most 192 MiB of HBM per device.

v0:
```python
import jax
import jax.numpy as jnp
from jax import lax
from jax.sharding import PartitionSpec as P

CB = 4


def passed_along(block, axis, distance):
    devices = range(lax.axis_size(axis))
    route = [((i - distance) % len(devices), i) for i in devices]
    return lax.ppermute(block, axis, route)


def local(block_values, block_columns, row_counts, prolong_blocks, aggregates):
    panel_length = row_counts.shape[0]
    slots_here = block_values.shape[1]
    slot_total = panel_length * slots_here
    block_size = block_values.shape[2]
    group_size = lax.axis_size("grp")
    panel_total = lax.axis_size("blk")
    coarse_count = CB * panel_total
    panel_blocks, panel_aggs = (
        lax.all_gather(prolong_blocks, "grp", axis=0, tiled=True),
        lax.all_gather(aggregates, "grp", axis=0, tiled=True),
    )
    lower = []
    upper = []
    going_down = (panel_blocks, panel_aggs)
    going_up = (panel_blocks, panel_aggs)
    for hop in range(2):
        going_down = passed_along((going_down[0], going_down[1]), "blk", 1)
        lower.insert(0, going_down)
        going_up = passed_along((going_up[0], going_up[1]), "blk", -1)
        upper.append(going_up)
    pieces = lower + [(panel_blocks, panel_aggs)] + upper
    window_blocks = jnp.concatenate([piece[0] for piece in pieces], axis=0)
    window_aggs = jnp.concatenate([piece[1] for piece in pieces], axis=0)
    own_blocks = window_blocks[2 * panel_length : 3 * panel_length]
    own_aggs = window_aggs[2 * panel_length : 3 * panel_length]
    wanted = block_columns.reshape(slot_total)
    column_panel = wanted // panel_length
    distance = jnp.mod(column_panel - lax.axis_index("blk") + 2, panel_total)
    local_rows = distance * panel_length + wanted % panel_length
    fetched = jnp.take(window_blocks, local_rows, axis=0)
    fetched_aggs = jnp.take(window_aggs, local_rows, axis=0)
    prolong_picked = fetched.reshape(panel_length, slots_here, block_size, block_size)
    product = jnp.einsum(
        "rkab,rkbc->rkac", block_values, prolong_picked, preferred_element_type=jnp.float32
    )
    slot_ids = lax.axis_index("grp") * slots_here + jnp.arange(slots_here, dtype=jnp.int32)
    live = slot_ids[None, :] < row_counts[:, None]
    product = jnp.where(live[:, :, None, None], product, 0.0).astype(jnp.bfloat16)
    restricted = jnp.einsum(
        "rba,rkbc->rkac", own_blocks, product, preferred_element_type=jnp.float32
    ).reshape(slot_total, block_size, block_size)
    local_coarse = own_aggs - lax.axis_index("blk") * CB
    target = fetched_aggs * CB + jnp.broadcast_to(
        local_coarse[:, None], (panel_length, slots_here)
    ).reshape(slot_total)
    share = coarse_count // group_size
    wanted_targets = jnp.arange(share * lax.axis_size("grp") * CB, dtype=jnp.int32)
    selector = (wanted_targets[:, None] == target[None, :]).astype(jnp.float32)
    summed = jnp.einsum(
        "ts,sab->tab",
        selector,
        restricted,
        precision=lax.Precision.HIGHEST,
        preferred_element_type=jnp.float32,
    )
    return lax.psum_scatter(
        summed.reshape(share * lax.axis_size("grp"), CB, block_size, block_size),
        "grp",
        scatter_dimension=0,
        tiled=True,
    )


def solution(mesh):
    return jax.shard_map(
        local,
        mesh=mesh,
        in_specs=(
            P("blk", "grp", None, None),
            P("blk", "grp"),
            P("blk"),
            P(("blk", "grp"), None, None),
            P(("blk", "grp")),
        ),
        out_specs=P("grp", "blk", None, None),
        check_vma=False,
    )
```

profile of v0, /device:TPU:0, one launch (start us, length us, event | category | flops | bytes accessed | tf_op | source)
XLA Modules:
  0.0 358.8 jit_solution(9059910426823162043)
XLA Ops:
  6.5 0.7 all-gather.2.cloned.1.call-update
  7.3 48.5 %all-gather.2.cloned.1.call-done = bf16[192,64,64]{2,1,0:T(8,128)(2,1)} async-done(((bf16[48,64,64]{2,1,0:T(8,128)(2,1)}), bf16[192,64,64]{2,1,0:T(8,128)(2,1)}) %all-gather.2.cloned.1.call-update) | async-done | bytes 1572880 | tf_op jit(solution)/shard_map/all_gather | solution.py:24
  55.8 4.2 %copy.25 = bf16[192,64,64]{0,2,1:T(8,128)(2,1)S(1)} copy(bf16[192,64,64]{2,1,0:T(8,128)(2,1)} %all-gather.2.cloned.1.call-done) | data formatting | bytes 3145728 | tf_op jit(solution)/shard_map/all_gather | solution.py:24
  60.1 3.5 collective-permute-start.6
  63.6 1.2 dynamic-slice
  65.5 0.9 dynamic-update-slice
  66.4 7.3 %all-reduce = s32[192]{0:T(256)S(1)} all-reduce(s32[192]{0:T(256)S(1)} %dynamic-update-slice), channel_id=1, replica_groups=mesh['blk'=8,'grp'=4] {'grp'}, use_global_device_ids=true, to_apply=%add | all-reduce | flops 192 | bytes 1536
  73.7 3.5 collective-permute-start.2
  77.2 30.8 %collective-permute-done.4 = bf16[192,64,64]{0,2,1:T(8,128)(2,1)} collective-permute-done((bf16[192,64,64]{0,2,1:T(8,128)(2,1)S(1)}, bf16[192,64,64]{0,2,1:T(8,128)(2,1)}, u32[]{:S(2)}, u32[]{:S(2)}) %collective-permute-start.4) | collective-permute-done | bytes 1572896 | tf_op jit(solution)/shard_map/ppermute | solution.py:12
  108.1 0.7 compare_and_fusion
  109.5 3.6 %collective-permute-start.7 = (bf16[192,64,64]{0,2,1:T(8,128)(2,1)}, bf16[192,64,64]{0,2,1:T(8,128)(2,1)}, u32[]{:S(2)}, u32[]{:S(2)}) collective-permute-start(bf16[192,64,64]{0,2,1:T(8,128)(2,1)} %collective-permute-done.6), channel_id=1, source_target_pairs={{4,0},{8,4},{12,8},{16,12},{20,16},{24,20},{28,24},{0,28},{5,1},{9... | collective-permute-start | bytes 4718600 | tf_op jit(solution)/shard_map/ppermute | solution.py:12
  113.9 0.8 broadcast_compare_fusion
  114.8 3.5 collective-permute-start.3
  119.0 17.1 %copy.32 = bf16[192,4,64,64]{3,2,1,0:T(8,128)(2,1)} copy(bf16[192,4,64,64]{0,3,2,1:T(8,128)(2,1)} %param.5) | data formatting | bytes 12582912 | tf_op args[0]
  136.1 21.3 %collective-permute-done.1 = s32[192]{0:T(256)S(1)} collective-permute-done((s32[192]{0:T(256)S(1)}, s32[192]{0:T(256)S(1)}, u32[]{:S(2)}, u32[]{:S(2)}) %collective-permute-start.1) | collective-permute-done | bytes 800 | tf_op jit(solution)/shard_map/ppermute | solution.py:12
  157.5 3.2 gather_fusion
  160.7 5.3 %copy.28 = bf16[192,64,64]{2,1,0:T(8,128)(2,1)} copy(bf16[192,64,64]{0,2,1:T(8,128)(2,1)} %collective-permute-done.4) | data formatting | bytes 3145728 | tf_op jit(solution)/shard_map/ppermute | solution.py:12
  166.0 5.3 %copy.29 = bf16[192,64,64]{2,1,0:T(8,128)(2,1)} copy(bf16[192,64,64]{0,2,1:T(8,128)(2,1)} %collective-permute-done.6) | data formatting | bytes 3145728 | tf_op jit(solution)/shard_map/ppermute | solution.py:12
  171.3 5.2 %copy.27 = bf16[192,64,64]{2,1,0:T(8,128)(2,1)} copy(bf16[192,64,64]{0,2,1:T(8,128)(2,1)} %collective-permute-done.5) | data formatting | bytes 3145728 | tf_op jit(solution)/shard_map/ppermute | solution.py:12
  176.5 4.4 %constant_dynamic-update-slice_fusion.4 = bf16[960,64,64]{2,1,0:T(8,128)(2,1)} fusion(bf16[192,64,64]{2,1,0:T(8,128)(2,1)} %copy.27), kind=kLoop, calls=%fused_computation.31 | loop fusion | bytes 4718592
  180.8 4.3 %constant_dynamic-update-slice_fusion.3 = bf16[960,64,64]{2,1,0:T(8,128)(2,1)} fusion(bf16[960,64,64]{2,1,0:T(8,128)(2,1)} %constant_dynamic-update-slice_fusion.4, bf16[192,64,64]{2,1,0:T(8,128)(2,1)} %copy.28), kind=kLoop, calls=%fused_computation.30 | loop fusion | bytes 6291456
  185.1 2.4 constant_dynamic-update-slice_fusion.2
  187.5 2.4 constant_dynamic-update-slice_fusion.1
  189.9 5.3 %copy.30 = bf16[192,64,64]{2,1,0:T(8,128)(2,1)} copy(bf16[192,64,64]{0,2,1:T(8,128)(2,1)} %collective-permute-done.7) | data formatting | bytes 3145728 | tf_op jit(solution)/shard_map/ppermute | solution.py:12
  195.1 4.2 %constant_dynamic-update-slice_fusion = bf16[960,64,64]{2,1,0:T(8,128)(2,1)} fusion(bf16[960,64,64]{2,1,0:T(8,128)(2,1)} %constant_dynamic-update-slice_fusion.1, bf16[192,64,64]{2,1,0:T(8,128)(2,1)} %copy.30), kind=kLoop, calls=%fused_computation.27 | loop fusion | bytes 6291456 | tf_op jit(solution)/shard_map/concatenate | solution.py:37
  199.3 25.3 %gather_fusion.1 = bf16[768,64,64]{2,1,0:T(8,128)(2,1)} fusion(bf16[960,64,64]{2,1,0:T(8,128)(2,1)} %constant_dynamic-update-slice_fusion, s32[1024]{0:T(1024)S(1)} %pad_clamp_fusion), kind=kCustom, calls=%fused_computation.1 | custom fusion | bytes 12585984 | tf_op jit(solution)/shard_map/jit(_take)/gather | solution.py:45
  224.6 16.6 %copy.31 = bf16[192,4,64,64]{2,3,1,0:T(8,128)(2,1)} copy(bf16[192,4,64,64]{3,2,1,0:T(8,128)(2,1)} %bitcast.23) | data formatting | bytes 12582912 | tf_op jit(solution)/shard_map/jit(_take)/gather | solution.py:45
  241.3 22.3 %fusion.1 = f32[192,4,64,64]{3,2,1,0:T(8,128)} fusion(pred[192,4]{1,0:T(8,128)(4,1)S(1)} %broadcast_compare_fusion, bf16[192,4,64,64]{3,2,1,0:T(8,128)(2,1)} %copy.32, bf16[192,4,64,64]{2,3,1,0:T(8,128)(2,1)} %copy.31, pred[192,4]{1,0:T(8,128)(4,1)S(1)} %copy.24, bf16[192,64,64]{2,1,0:T(8,128)(2,1)S(1)} %copy-done), kind=kOutput, calls=%fused_computation.4 | convolution fusion | flops 814743552 | bytes 26740224 | tf_op jit(solution)/shard_map/rba,rkbc->rkac/dot_general | solution.py:54
  263.6 22.3 %copy.33 = f32[768,64,64]{0,2,1:T(8,128)} copy(f32[768,64,64]{1,2,0:T(8,128)} %bitcast.22) | data formatting | bytes 25165824 | tf_op jit(solution)/shard_map/reshape | solution.py:56
  285.9 13.4 %fusion.3 = f32[32,4,64,64]{3,0,2,1:T(8,128)} fusion(f32[768,64,64]{0,2,1:T(8,128)} %copy.33, s32[768]{0:T(1024)S(1)} %multiply_add_fusion, s32[32,4]{0,1:T(4,128)S(1)} %multiply_add_fusion.1), kind=kOutput, calls=%fused_computation.5 | convolution fusion | flops 4831936512 | bytes 14683648 | tf_op jit(solution)/shard_map/ts,sab->tab/dot_general | solution.py:64
  299.3 50.2 %reduce-scatter.2.cloned.1.call-done = f32[8,4,64,64]{3,0,2,1:T(8,128)} async-done(((f32[32,4,64,64]{3,0,2,1:T(8,128)}), f32[8,4,64,64]{3,0,2,1:T(8,128)}) %reduce-scatter.2.cloned.1.call-update) | async-done | bytes 524304 | tf_op jit(solution)/shard_map/reduce_scatter | solution.py:71
  349.5 2.4 copy.34
  (38 shorter events, 2.5 us)
Async XLA Ops:
  6.5 49.2 %all-gather.2.cloned.1.call-start = ((), (), s32[]{:S(2)}) async-start(), calls=%async_computation.1 | async-start | bytes 3932160 | tf_op jit(solution)/shard_map/all_gather | solution.py:24
  7.3 342.3 %reduce-scatter.2.cloned.1.call-start = ((), (), s32[]{:S(2)}) async-start(), calls=%async_computation.2 | async-start | bytes 5242880 | tf_op jit(solution)/shard_map/reduce_scatter | solution.py:71
  60.0 48.1 %collective-permute-start.4 = (bf16[192,64,64]{0,2,1:T(8,128)(2,1)S(1)}, bf16[192,64,64]{0,2,1:T(8,128)(2,1)}, u32[]{:S(2)}, u32[]{:S(2)}) collective-permute-start(bf16[192,64,64]{0,2,1:T(8,128)(2,1)S(1)} %copy.25), channel_id=1, source_target_pairs={{28,0},{0,4},{4,8},{8,12},{12,16},{16,20},{20,24},{24,28},{29,1},{... | collective-permute-start | bytes 4718600 | tf_op jit(solution)/shard_map/ppermute | solution.py:12
  60.1 49.4 %collective-permute-start.6 = (bf16[192,64,64]{0,2,1:T(8,128)(2,1)S(1)}, bf16[192,64,64]{0,2,1:T(8,128)(2,1)}, u32[]{:S(2)}, u32[]{:S(2)}) collective-permute-start(bf16[192,64,64]{0,2,1:T(8,128)(2,1)S(1)} %copy.25), channel_id=1, source_target_pairs={{4,0},{8,4},{12,8},{16,12},{20,16},{24,20},{28,24},{0,28},{5,1},{9... | collective-permute-start | bytes 4718600 | tf_op jit(solution)/shard_map/ppermute | solution.py:12
  73.7 41.0 %collective-permute-start = (s32[192]{0:T(256)S(1)}, s32[192]{0:T(256)S(1)}, u32[]{:S(2)}, u32[]{:S(2)}) collective-permute-start(s32[192]{0:T(256)S(1)} %all-reduce), channel_id=1, source_target_pairs={{28,0},{0,4},{4,8},{8,12},{12,16},{16,20},{20,24},{24,28},{29,1},{... | collective-permute-start | bytes 2312 | tf_op jit(solution)/shard_map/ppermute | solution.py:12
  73.7 41.1 %collective-permute-start.2 = (s32[192]{0:T(256)S(1)}, s32[192]{0:T(256)S(1)}, u32[]{:S(2)}, u32[]{:S(2)}) collective-permute-start(s32[192]{0:T(256)S(1)} %all-reduce), channel_id=1, source_target_pairs={{4,0},{8,4},{12,8},{16,12},{20,16},{24,20},{28,24},{0,28},{5,1},{9... | collective-permute-start | bytes 2312 | tf_op jit(solution)/shard_map/ppermute | solution.py:12
  108.1 63.2 %collective-permute-start.5 = (bf16[192,64,64]{0,2,1:T(8,128)(2,1)}, bf16[192,64,64]{0,2,1:T(8,128)(2,1)}, u32[]{:S(2)}, u32[]{:S(2)}) collective-permute-start(bf16[192,64,64]{0,2,1:T(8,128)(2,1)} %collective-permute-done.4), channel_id=1, source_target_pairs={{28,0},{0,4},{4,8},{8,12},{12,16},{16,20},{20,24},{24,28},{29,1},{... | collective-permute-start | bytes 4718600 | tf_op jit(solution)/shard_map/ppermute | solution.py:12
  109.5 80.4 %collective-permute-start.7 = (bf16[192,64,64]{0,2,1:T(8,128)(2,1)}, bf16[192,64,64]{0,2,1:T(8,128)(2,1)}, u32[]{:S(2)}, u32[]{:S(2)}) collective-permute-start(bf16[192,64,64]{0,2,1:T(8,128)(2,1)} %collective-permute-done.6), channel_id=1, source_target_pairs={{4,0},{8,4},{12,8},{16,12},{20,16},{24,20},{28,24},{0,28},{5,1},{9... | collective-permute-start | bytes 4718600 | tf_op jit(solution)/shard_map/ppermute | solution.py:12
  114.7 42.7 %collective-permute-start.1 = (s32[192]{0:T(256)S(1)}, s32[192]{0:T(256)S(1)}, u32[]{:S(2)}, u32[]{:S(2)}) collective-permute-start(s32[192]{0:T(256)S(1)} %collective-permute-done), channel_id=1, source_target_pairs={{28,0},{0,4},{4,8},{8,12},{12,16},{16,20},{20,24},{24,28},{29,1},{... | collective-permute-start | bytes 2312 | tf_op jit(solution)/shard_map/ppermute | solution.py:12
  114.8 42.6 %collective-permute-start.3 = (s32[192]{0:T(256)S(1)}, s32[192]{0:T(256)S(1)}, u32[]{:S(2)}, u32[]{:S(2)}) collective-permute-start(s32[192]{0:T(256)S(1)} %collective-permute-done.2), channel_id=1, source_target_pairs={{4,0},{8,4},{12,8},{16,12},{20,16},{24,20},{28,24},{0,28},{5,1},{9... | collective-permute-start | bytes 2312 | tf_op jit(solution)/shard_map/ppermute | solution.py:12
  166.0 19.1 %copy-start = (bf16[192,64,64]{2,1,0:T(8,128)(2,1)S(1)}, bf16[192,64,64]{2,1,0:T(8,128)(2,1)}, u32[]{:S(2)}) copy-start(bf16[192,64,64]{2,1,0:T(8,128)(2,1)} %all-gather.2.cloned.1.call-done) | copy-start | bytes 4718596
  176.5 11.0 %copy-start.1 = (bf16[192,64,64]{2,1,0:T(8,128)(2,1)S(1)}, bf16[192,64,64]{2,1,0:T(8,128)(2,1)}, u32[]{:S(2)}) copy-start(bf16[192,64,64]{2,1,0:T(8,128)(2,1)} %copy.29) | copy-start | bytes 4718596
Sparse Core Ops, SparseCore 0:
  9.2 46.5 all-gather.1
  299.5 50.0 reduce-scatter.1
where the time goes:
time: 361 us; the launch traced here: 359 us
  waiting for transfers between devices  152 us (42%)
  local copies, waits for them, and re-layouts  133 us (37%)
  matrix products  35.7 us (10%)
  starting transfers between devices  14.3 us (4%)
  between operations  14.2 us (4%)
  blocking collectives  7.32 us (2%)
    ppermute x8, waiting for transfers between devices, passed_along(): return lax.ppermute(block, axis, route)  52.2 us
    reduce_scatter x1, waiting for transfers between devices, local(): lax.psum_scatter(summed.reshape(share * lax.axis_size('grp'), CB, block_s...  50.2 us
    all_gather x1, waiting for transfers between devices, local(): lax.all_gather(prolong_blocks, 'grp', axis=0, tiled=True)  48.5 us
    gather x2, local copies, waits for them, and re-layouts, local(): fetched = jnp.take(window_blocks, local_rows, axis=0)  41.9 us
    unnamed x12, local copies, waits for them, and re-layouts  32.5 us
    dot_general x1, matrix products, local(): jnp.einsum('rba,rkbc->rkac', own_blocks, product, preferred_element_type=...  22.3 us
    reshape x1, local copies, waits for them, and re-layouts, local(): restricted = jnp.einsum('rba,rkbc->rkac', own_blocks, product, preferred_...  22.3 us
    ppermute x4, local copies, waits for them, and re-layouts, passed_along(): return lax.ppermute(block, axis, route)  21 us
  transfers between devices with their start and end apart: 10, of which 4 were waited for; matrix products, arithmetic and copies ran while one was open for 15% of the time, Pallas kernels for 0%

commit v1 on v0

--- a/solution.py
+++ b/solution.py
@@ -4,6 +4,24 @@
 from jax.sharding import PartitionSpec as P
 
 CB = 4
+
+
+def collect(value, axis, dim):
+    ways, here, step = (lax.axis_size(axis), lax.axis_index(axis), value.shape[dim])
+    shape = [n * ways if d == dim else n for d, n in enumerate(value.shape)]
+    full = lax.dynamic_update_slice_in_dim(
+        jnp.zeros(shape, value.dtype), value, here * step, axis=dim
+    )
+    going_up = going_down = value
+    for far in range(1, ways // 2 + 1):
+        going_up = lax.ppermute(going_up, axis, [(d, (d + 1) % ways) for d in range(ways)])
+        full = lax.dynamic_update_slice_in_dim(full, going_up, (here - far) % ways * step, axis=dim)
+        if 2 * far < ways:
+            going_down = lax.ppermute(going_down, axis, [(d, (d - 1) % ways) for d in range(ways)])
+            full = lax.dynamic_update_slice_in_dim(
+                full, going_down, (here + far) % ways * step, axis=dim
+            )
+    return full
 
 
 def passed_along(block, axis, distance):
@@ -21,7 +39,7 @@
     panel_total = lax.axis_size("blk")
     coarse_count = CB * panel_total
     panel_blocks, panel_aggs = (
-        lax.all_gather(prolong_blocks, "grp", axis=0, tiled=True),
+        collect(prolong_blocks, "grp", 0),
         lax.all_gather(aggregates, "grp", axis=0, tiled=True),
     )
     lower = []

time: 361 us -> 352 us (0.975)
  local copies, waits for them, and re-layouts: 133 us -> 120 us
  waiting for transfers between devices: 152 us -> 159 us
    all_gather x1 -> x0, waiting for transfers between devices: 48.5 us -> none  [local(): lax.all_gather(prolong_blocks, 'grp', axis=0, tiled=True)]
    ppermute x0 -> x3, waiting for transfers between devices: none -> 45.8 us  [the longest x2 32.8 us: collect(): lax.ppermute(going_up, axis, [(d, (d + 1) % ways) for d in range(ways)])]
    gather x2 -> x1, local copies, waits for them, and re-layouts: 41.9 us -> 25.3 us  [local(): fetched = jnp.take(window_blocks, local_rows, axis=0)]
    dynamic_update_slice x0 -> x5, local copies, waits for them, and re-layouts: none -> 7.65 us  [the longest x3 5.17 us: collect(): lax.dynamic_update_slice_in_dim(full, going_up, (here - far) % ways * ste...]
    ppermute x8, waiting for transfers between devices: 52.2 us -> 58.5 us  [passed_along(): return lax.ppermute(block, axis, route)]
    ppermute x8, starting transfers between devices: 14.3 us -> 8.58 us  [passed_along(): return lax.ppermute(block, axis, route)]
    ppermute x0 -> x3, starting transfers between devices: none -> 5.1 us  [the longest x2 4.08 us: collect(): lax.ppermute(going_up, axis, [(d, (d + 1) % ways) for d in range(ways)])]
    reduce_scatter x1, waiting for transfers between devices: 50.2 us -> 54.9 us  [local(): lax.psum_scatter(summed.reshape(share * lax.axis_size('grp'), CB, block_s...]
  transfers between devices with their start and end apart: 10 -> 12, of which waited for: 4 -> 7; matrix products, arithmetic and copies ran while one was open for 15% -> 16% of each run, Pallas kernels for 0% -> 0%
where the time goes in v1:
time: 352 us; the launch traced here: 351 us
  waiting for transfers between devices  159 us (45%)
  local copies, waits for them, and re-layouts  120 us (34%)
  matrix products  36.3 us (10%)
  between operations  14.2 us (4%)
  starting transfers between devices  13.7 us (4%)
  blocking collectives  7.56 us (2%)
    ppermute x8, waiting for transfers between devices, passed_along(): return lax.ppermute(block, axis, route)  58.5 us
    reduce_scatter x1, waiting for transfers between devices, local(): lax.psum_scatter(summed.reshape(share * lax.axis_size('grp'), CB, block_s...  54.9 us
    ppermute x2, waiting for transfers between devices, collect(): lax.ppermute(going_up, axis, [(d, (d + 1) % ways) for d in range(ways)])  32.8 us
    unnamed x18, local copies, waits for them, and re-layouts  31.2 us
    gather x1, local copies, waits for them, and re-layouts, local(): fetched = jnp.take(window_blocks, local_rows, axis=0)  25.3 us
    dot_general x1, matrix products, local(): jnp.einsum('rba,rkbc->rkac', own_blocks, product, preferred_element_type=...  22.9 us
    reshape x1, local copies, waits for them, and re-layouts, local(): restricted = jnp.einsum('rba,rkbc->rkac', own_blocks, product, preferred_...  22.4 us
    ppermute x4, local copies, waits for them, and re-layouts, passed_along(): return lax.ppermute(block, axis, route)  20.9 us
  transfers between devices with their start and end apart: 12, of which 7 were waited for; matrix products, arithmetic and copies ran while one was open for 16% of the time, Pallas kernels for 0%

profile of v1, /device:TPU:0, one launch (start us, length us, event | category | flops | bytes accessed | tf_op | source)
XLA Modules:
  0.0 350.9 jit_solution(5824317539116562510)
XLA Ops:
  6.6 3.0 collective-permute-start.4
  10.6 18.6 %collective-permute-done.4 = bf16[48,64,64]{2,1,0:T(8,128)(2,1)} collective-permute-done((bf16[48,64,64]{2,1,0:T(8,128)(2,1)}, bf16[48,64,64]{2,1,0:T(8,128)(2,1)}, u32[]{:S(2)}, u32[]{:S(2)}) %collective-permute-start.4) | collective-permute-done | bytes 393248 | tf_op jit(solution)/shard_map/ppermute | solution.py:17
  29.3 1.1 collective-permute-start.6
  31.1 1.2 constant_dynamic-update-slice_fusion.8
  32.4 1.2 constant_dynamic-update-slice_fusion.7
  33.6 13.0 %collective-permute-done.5 = bf16[48,64,64]{2,1,0:T(8,128)(2,1)} collective-permute-done((bf16[48,64,64]{2,1,0:T(8,128)(2,1)}, bf16[48,64,64]{2,1,0:T(8,128)(2,1)}, u32[]{:S(2)}, u32[]{:S(2)}) %collective-permute-start.5) | collective-permute-done | bytes 393248 | tf_op jit(solution)/shard_map/ppermute | solution.py:20
  46.6 1.2 constant_dynamic-update-slice_fusion.6
  47.9 14.1 %collective-permute-done.6 = bf16[48,64,64]{2,1,0:T(8,128)(2,1)S(1)} collective-permute-done((bf16[48,64,64]{2,1,0:T(8,128)(2,1)}, bf16[48,64,64]{2,1,0:T(8,128)(2,1)S(1)}, u32[]{:S(2)}, u32[]{:S(2)}) %collective-permute-start.6) | collective-permute-done | bytes 393248 | tf_op jit(solution)/shard_map/ppermute | solution.py:17
  62.1 3.8 %copy.40 = bf16[192,64,64]{0,2,1:T(8,128)(2,1)} copy(bf16[192,64,64]{2,1,0:T(8,128)(2,1)S(1)} %constant_dynamic-update-slice_fusion.5) | data formatting | bytes 3145728 | tf_op jit(solution)/shard_map/dynamic_update_slice | solution.py:18
  66.0 3.5 %collective-permute-start.9 = (bf16[192,64,64]{0,2,1:T(8,128)(2,1)}, bf16[192,64,64]{0,2,1:T(8,128)(2,1)}, u32[]{:S(2)}, u32[]{:S(2)}) collective-permute-start(bf16[192,64,64]{0,2,1:T(8,128)(2,1)} %copy.40), channel_id=1, source_target_pairs={{4,0},{8,4},{12,8},{16,12},{20,16},{24,20},{28,24},{0,28},{5,1},{9... | collective-permute-start | bytes 4718600 | tf_op jit(solution)/shard_map/ppermute | solution.py:30
  71.0 7.6 %all-reduce = s32[192]{0:T(256)S(1)} all-reduce(s32[192]{0:T(256)S(1)} %dynamic-update-slice), channel_id=1, replica_groups=mesh['blk'=8,'grp'=4] {'grp'}, use_global_device_ids=true, to_apply=%add | all-reduce | flops 192 | bytes 1536
  79.1 34.6 %collective-permute-done.7 = bf16[192,64,64]{0,2,1:T(8,128)(2,1)} collective-permute-done((bf16[192,64,64]{0,2,1:T(8,128)(2,1)}, bf16[192,64,64]{0,2,1:T(8,128)(2,1)}, u32[]{:S(2)}, u32[]{:S(2)}) %collective-permute-start.7) | collective-permute-done | bytes 1572896 | tf_op jit(solution)/shard_map/ppermute | solution.py:30
  113.8 3.6 %collective-permute-start.10 = (bf16[192,64,64]{0,2,1:T(8,128)(2,1)}, bf16[192,64,64]{0,2,1:T(8,128)(2,1)}, u32[]{:S(2)}, u32[]{:S(2)}) collective-permute-start(bf16[192,64,64]{0,2,1:T(8,128)(2,1)} %collective-permute-done.9), channel_id=1, source_target_pairs={{4,0},{8,4},{12,8},{16,12},{20,16},{24,20},{28,24},{0,28},{5,1},{9... | collective-permute-start | bytes 4718600 | tf_op jit(solution)/shard_map/ppermute | solution.py:30
  120.0 17.1 %copy.47 = bf16[192,4,64,64]{3,2,1,0:T(8,128)(2,1)} copy(bf16[192,4,64,64]{0,3,2,1:T(8,128)(2,1)} %param.5) | data formatting | bytes 12582912 | tf_op args[0]
  137.0 22.4 %collective-permute-done.3 = s32[192]{0:T(256)S(1)} collective-permute-done((s32[192]{0:T(256)S(1)}, s32[192]{0:T(256)S(1)}, u32[]{:S(2)}, u32[]{:S(2)}) %collective-permute-start.3) | collective-permute-done | bytes 800 | tf_op jit(solution)/shard_map/ppermute | solution.py:30
  159.4 1.5 collective-permute-done.1
  161.0 3.2 gather_fusion
  164.2 5.2 %copy.43 = bf16[192,64,64]{2,1,0:T(8,128)(2,1)} copy(bf16[192,64,64]{0,2,1:T(8,128)(2,1)} %collective-permute-done.7) | data formatting | bytes 3145728 | tf_op jit(solution)/shard_map/ppermute | solution.py:30
  169.4 5.3 %copy.44 = bf16[192,64,64]{2,1,0:T(8,128)(2,1)} copy(bf16[192,64,64]{0,2,1:T(8,128)(2,1)} %collective-permute-done.9) | data formatting | bytes 3145728 | tf_op jit(solution)/shard_map/ppermute | solution.py:30
  174.6 5.3 %copy.42 = bf16[192,64,64]{2,1,0:T(8,128)(2,1)} copy(bf16[192,64,64]{0,2,1:T(8,128)(2,1)} %collective-permute-done.8) | data formatting | bytes 3145728 | tf_op jit(solution)/shard_map/ppermute | solution.py:30
  179.9 4.4 %constant_dynamic-update-slice_fusion.4 = bf16[960,64,64]{2,1,0:T(8,128)(2,1)} fusion(bf16[192,64,64]{2,1,0:T(8,128)(2,1)} %copy.42), kind=kLoop, calls=%fused_computation.31 | loop fusion | bytes 4718592
  184.3 4.2 %constant_dynamic-update-slice_fusion.3 = bf16[960,64,64]{2,1,0:T(8,128)(2,1)} fusion(bf16[960,64,64]{2,1,0:T(8,128)(2,1)} %constant_dynamic-update-slice_fusion.4, bf16[192,64,64]{2,1,0:T(8,128)(2,1)} %copy.43), kind=kLoop, calls=%fused_computation.30 | loop fusion | bytes 6291456
  188.5 2.4 constant_dynamic-update-slice_fusion.2
  190.9 2.3 constant_dynamic-update-slice_fusion.1
  193.3 5.3 %copy.45 = bf16[192,64,64]{2,1,0:T(8,128)(2,1)} copy(bf16[192,64,64]{0,2,1:T(8,128)(2,1)} %collective-permute-done.10) | data formatting | bytes 3145728 | tf_op jit(solution)/shard_map/ppermute | solution.py:30
  198.5 4.2 %constant_dynamic-update-slice_fusion = bf16[960,64,64]{2,1,0:T(8,128)(2,1)} fusion(bf16[960,64,64]{2,1,0:T(8,128)(2,1)} %constant_dynamic-update-slice_fusion.1, bf16[192,64,64]{2,1,0:T(8,128)(2,1)} %copy.45), kind=kLoop, calls=%fused_computation.27 | loop fusion | bytes 6291456 | tf_op jit(solution)/shard_map/concatenate | solution.py:55
  202.7 25.3 %gather_fusion.1 = bf16[768,64,64]{2,1,0:T(8,128)(2,1)} fusion(bf16[960,64,64]{2,1,0:T(8,128)(2,1)} %constant_dynamic-update-slice_fusion, s32[1024]{0:T(1024)S(1)} %pad_clamp_fusion), kind=kCustom, calls=%fused_computation.1 | custom fusion | bytes 12585984 | tf_op jit(solution)/shard_map/jit(_take)/gather | solution.py:63
  228.0 22.9 %fusion.1 = f32[192,4,64,64]{3,2,1,0:T(8,128)} fusion(pred[192,4]{1,0:T(8,128)(4,1)S(1)} %broadcast_compare_fusion, bf16[192,4,64,64]{3,2,1,0:T(8,128)(2,1)} %copy.47, bf16[192,4,64,64]{3,2,1,0:T(8,128)(2,1)} %bitcast.23, pred[192,4]{1,0:T(8,128)(4,1)S(1)} %copy.39, bf16[192,64,64]{2,1,0:T(8,128)(2,1)S(1)} %constant_dynamic-update-slice_fusion.5), kind=kOutput, calls=%fused_computation.4 | convolution fusion | flops 814743552 | bytes 26740224 | tf_op jit(solution)/shard_map/rba,rkbc->rkac/dot_general | solution.py:72
  251.0 22.4 %copy.48 = f32[768,64,64]{0,2,1:T(8,128)} copy(f32[768,64,64]{1,2,0:T(8,128)} %bitcast.22) | data formatting | bytes 25165824 | tf_op jit(solution)/shard_map/reshape | solution.py:74
  273.3 13.4 %fusion.3 = f32[32,4,64,64]{3,0,2,1:T(8,128)} fusion(f32[768,64,64]{0,2,1:T(8,128)} %copy.48, s32[768]{0:T(1024)S(1)} %multiply_add_fusion, s32[32,4]{0,1:T(4,128)S(1)} %multiply_add_fusion.1), kind=kOutput, calls=%fused_computation.5 | convolution fusion | flops 4831936512 | bytes 14683648 | tf_op jit(solution)/shard_map/ts,sab->tab/dot_general | solution.py:82
  286.8 54.9 %reduce-scatter.2.cloned.1.call-done = f32[8,4,64,64]{3,0,2,1:T(8,128)} async-done(((f32[32,4,64,64]{3,0,2,1:T(8,128)}), f32[8,4,64,64]{3,0,2,1:T(8,128)}) %reduce-scatter.2.cloned.1.call-update) | async-done | bytes 524304 | tf_op jit(solution)/shard_map/reduce_scatter | solution.py:89
  341.6 2.4 copy.49
  (51 shorter events, 6.0 us)
Async XLA Ops:
  6.5 63.0 %copy-start.4 = (u32[32]{0:T(128)S(1)}, u32[32]{0:T(128)}, u32[]{:S(2)}) copy-start(u32[32]{0:T(128)} %constant.113) | copy-start | bytes 388
  6.5 64.2 %copy-start.3 = (s32[48]{0:T(128)S(1)}, s32[48]{0:T(128)}, u32[]{:S(2)}) copy-start(s32[48]{0:T(128)} %param.9) | copy-start | bytes 580
  6.5 107.2 %copy-start.1 = (s32[192,4]{0,1:T(4,128)S(1)}, s32[192,4]{0,1:T(4,128)}, u32[]{:S(2)}) copy-start(s32[192,4]{0,1:T(4,128)} %param.6) | copy-start | bytes 9220
  6.5 111.7 %copy-start.2 = (s32[192]{0:T(256)S(1)}, s32[192]{0:T(256)}, u32[]{:S(2)}) copy-start(s32[192]{0:T(256)} %param.7) | copy-start | bytes 2308
  6.5 335.1 %reduce-scatter.2.cloned.1.call-start = ((), (), s32[]{:S(2)}) async-start(), calls=%async_computation.1 | async-start | bytes 5242880 | tf_op jit(solution)/shard_map/reduce_scatter | solution.py:89
  6.6 22.7 %collective-permute-start.4 = (bf16[48,64,64]{2,1,0:T(8,128)(2,1)}, bf16[48,64,64]{2,1,0:T(8,128)(2,1)}, u32[]{:S(2)}, u32[]{:S(2)}) collective-permute-start(bf16[48,64,64]{2,1,0:T(8,128)(2,1)} %param.8), channel_id=1, source_target_pairs={{0,1},{1,2},{2,3},{3,0},{4,5},{5,6},{6,7},{7,4},{8,9},{9,10},{10,1... | collective-permute-start | bytes 1179656 | tf_op jit(solution)/shard_map/ppermute | solution.py:17
  9.6 37.0 %collective-permute-start.5 = (bf16[48,64,64]{2,1,0:T(8,128)(2,1)}, bf16[48,64,64]{2,1,0:T(8,128)(2,1)}, u32[]{:S(2)}, u32[]{:S(2)}) collective-permute-start(bf16[48,64,64]{2,1,0:T(8,128)(2,1)} %param.8), channel_id=1, source_target_pairs={{0,3},{1,0},{2,1},{3,2},{4,7},{5,4},{6,5},{7,6},{8,11},{9,8},{10,9... | collective-permute-start | bytes 1179656 | tf_op jit(solution)/shard_map/ppermute | solution.py:20
  29.3 32.8 %collective-permute-start.6 = (bf16[48,64,64]{2,1,0:T(8,128)(2,1)}, bf16[48,64,64]{2,1,0:T(8,128)(2,1)S(1)}, u32[]{:S(2)}, u32[]{:S(2)}) collective-permute-start(bf16[48,64,64]{2,1,0:T(8,128)(2,1)} %collective-permute-done.4), channel_id=1, source_target_pairs={{0,1},{1,2},{2,3},{3,0},{4,5},{5,6},{6,7},{7,4},{8,9},{9,10},{10,1... | collective-permute-start | bytes 1179656 | tf_op jit(solution)/shard_map/ppermute | solution.py:17
  66.0 47.8 %collective-permute-start.7 = (bf16[192,64,64]{0,2,1:T(8,128)(2,1)}, bf16[192,64,64]{0,2,1:T(8,128)(2,1)}, u32[]{:S(2)}, u32[]{:S(2)}) collective-permute-start(bf16[192,64,64]{0,2,1:T(8,128)(2,1)} %copy.40), channel_id=1, source_target_pairs={{28,0},{0,4},{4,8},{8,12},{12,16},{16,20},{20,24},{24,28},{29,1},{... | collective-permute-start | bytes 4718600 | tf_op jit(solution)/shard_map/ppermute | solution.py:30
  66.0 47.8 %collective-permute-start.9 = (bf16[192,64,64]{0,2,1:T(8,128)(2,1)}, bf16[192,64,64]{0,2,1:T(8,128)(2,1)}, u32[]{:S(2)}, u32[]{:S(2)}) collective-permute-start(bf16[192,64,64]{0,2,1:T(8,128)(2,1)} %copy.40), channel_id=1, source_target_pairs={{4,0},{8,4},{12,8},{16,12},{20,16},{24,20},{28,24},{0,28},{5,1},{9... | collective-permute-start | bytes 4718600 | tf_op jit(solution)/shard_map/ppermute | solution.py:30
  78.6 39.8 %collective-permute-start.2 = (s32[192]{0:T(256)S(1)}, s32[192]{0:T(256)S(1)}, u32[]{:S(2)}, u32[]{:S(2)}) collective-permute-start(s32[192]{0:T(256)S(1)} %all-reduce), channel_id=1, source_target_pairs={{4,0},{8,4},{12,8},{16,12},{20,16},{24,20},{28,24},{0,28},{5,1},{9... | collective-permute-start | bytes 2312 | tf_op jit(solution)/shard_map/ppermute | solution.py:30
  78.6 40.7 %collective-permute-start = (s32[192]{0:T(256)S(1)}, s32[192]{0:T(256)S(1)}, u32[]{:S(2)}, u32[]{:S(2)}) collective-permute-start(s32[192]{0:T(256)S(1)} %all-reduce), channel_id=1, source_target_pairs={{28,0},{0,4},{4,8},{8,12},{12,16},{16,20},{20,24},{24,28},{29,1},{... | collective-permute-start | bytes 2312 | tf_op jit(solution)/shard_map/ppermute | solution.py:30
  113.7 60.9 %collective-permute-start.8 = (bf16[192,64,64]{0,2,1:T(8,128)(2,1)}, bf16[192,64,64]{0,2,1:T(8,128)(2,1)}, u32[]{:S(2)}, u32[]{:S(2)}) collective-permute-start(bf16[192,64,64]{0,2,1:T(8,128)(2,1)} %collective-permute-done.7), channel_id=1, source_target_pairs={{28,0},{0,4},{4,8},{8,12},{12,16},{16,20},{20,24},{24,28},{29,1},{... | collective-permute-start | bytes 4718600 | tf_op jit(solution)/shard_map/ppermute | solution.py:30
  113.8 79.5 %collective-permute-start.10 = (bf16[192,64,64]{0,2,1:T(8,128)(2,1)}, bf16[192,64,64]{0,2,1:T(8,128)(2,1)}, u32[]{:S(2)}, u32[]{:S(2)}) collective-permute-start(bf16[192,64,64]{0,2,1:T(8,128)(2,1)} %collective-permute-done.9), channel_id=1, source_target_pairs={{4,0},{8,4},{12,8},{16,12},{20,16},{24,20},{28,24},{0,28},{5,1},{9... | collective-permute-start | bytes 4718600 | tf_op jit(solution)/shard_map/ppermute | solution.py:30
  118.3 41.1 %collective-permute-start.3 = (s32[192]{0:T(256)S(1)}, s32[192]{0:T(256)S(1)}, u32[]{:S(2)}, u32[]{:S(2)}) collective-permute-start(s32[192]{0:T(256)S(1)} %collective-permute-done.2), channel_id=1, source_target_pairs={{4,0},{8,4},{12,8},{16,12},{20,16},{24,20},{28,24},{0,28},{5,1},{9... | collective-permute-start | bytes 2312 | tf_op jit(solution)/shard_map/ppermute | solution.py:30
  119.3 41.7 %collective-permute-start.1 = (s32[192]{0:T(256)S(1)}, s32[192]{0:T(256)S(1)}, u32[]{:S(2)}, u32[]{:S(2)}) collective-permute-start(s32[192]{0:T(256)S(1)} %collective-permute-done), channel_id=1, source_target_pairs={{28,0},{0,4},{4,8},{8,12},{12,16},{16,20},{20,24},{24,28},{29,1},{... | collective-permute-start | bytes 2312 | tf_op jit(solution)/shard_map/ppermute | solution.py:30
  179.9 11.0 %copy-start = (bf16[192,64,64]{2,1,0:T(8,128)(2,1)S(1)}, bf16[192,64,64]{2,1,0:T(8,128)(2,1)}, u32[]{:S(2)}) copy-start(bf16[192,64,64]{2,1,0:T(8,128)(2,1)} %copy.44) | copy-start | bytes 4718596
Sparse Core Ops, SparseCore 0:
  286.9 54.6 reduce-scatter.1
